TPU v7x, 512 devices: a whole 4x4x16 slice. The times are simulated.
512 devices in a mesh: section: 32 (over z_lo, y, core), seq: 16 (over x, z_hi).
Axes of the slice: x: 4, y: 4, z: 16 (z_hi: 4, z_lo: 4; z = z_hi * 4 + z_lo), core: 2. Of those that a mesh axis runs over, the one named last changes fastest.
Arguments:
- up_activation: bfloat16 [32, 2048, 4096], P('section', 'seq'), as said below
- saved_projections: bfloat16 [32, 2048, 768], P('section', 'seq'), as said below
- up_cotangent: bfloat16 [32, 2048, 4096], P('section', 'seq'), may hold values from -6 to 6
- up_input_weight: bfloat16 [32, 4096, 768], P('section', 'seq'), may hold values from -0.09375 to 0.09375
- up_output_weight: bfloat16 [32, 512, 4096], P('section', None, 'seq'), may hold values from -0.25 to 0.25
- upward_gain: float32 [32, 4096], P('section'), may hold values from 0.5 to 1.5
- accum_input: bfloat16 [32, 4096, 768], P('section', 'seq'), may hold values from -48 to 48
- doc_starts: int32 [32, 2048], P('section', 'seq'), may hold values from 0 to 2047, as said below
Outputs:
- upward_grad: bfloat16 [32, 2048, 4096], P('section', 'seq')
- project_grads: bfloat16 [32, 4096, 768], P('section', 'seq')
Inputs may be any that keep to these rules, and one draw needn't show every extreme that they name: doc_starts[s, t] is the position of the first token of the document holding token t: it is 0 at t = 0, equals t or doc_starts[s, t - 1] elsewhere, and the last token of every micro-batch starts a document. `up_activation`: saved inputs of the upward layers. `saved_projections`: saved queries, keys and values of the upward layers.
All inputs are finite; a program needn't handle non-finite values.
Results may differ from a plain program's by a relative error of at most 0.014.
Values may be sent and summed in bfloat16 or wider, within the bound.
No kernel may reach another device: no remote copies, remote signals or barrier semaphores. Data moves between devices by JAX's collectives and lax.ppermute only.
A program may use at most 64 MiB of HBM per device.

v0:
```python
import jax
import jax.numpy as jnp
from jax import lax
from jax.sharding import PartitionSpec as P

HEAD = 128
GROUP = 4


def shifted(value, axis, steps):
    count = lax.axis_size(axis)
    initial, last = (max(0, -steps), min(count, count - steps))
    return lax.ppermute(value, axis, [(source, source + steps) for source in range(initial, last)])


def from_partner(x, axis, stride):
    return lax.ppermute(x, axis, [(i, i ^ 1 << stride) for i in range(lax.axis_size(axis))])


def contract_last(left, right):
    return lax.dot_general(
        left, right, (((1,), (1,)), ((), ())), preferred_element_type=jnp.float32
    )


def contract_first(left, right):
    return lax.dot_general(
        left, right, (((0,), (0,)), ((), ())), preferred_element_type=jnp.float32
    )


def normalize(values, gain):
    floats = values.astype(jnp.float32)
    inverse = lax.rsqrt(jnp.mean(floats * floats, axis=-1, keepdims=True) + 1e-05)
    unit = floats * inverse
    return (unit, inverse, unit * gain)


def per_device(
    up_activation,
    saved_projections,
    up_cotangent,
    up_input_weight,
    up_output_weight,
    upward_gain,
    accum_input,
    doc_starts,
):
    factor = HEAD ** (-0.5)
    width = GROUP * HEAD
    count = up_activation.shape[1]
    first = lax.axis_index("seq") * count
    saved = saved_projections[0]
    cotangent = up_cotangent[0]
    unit_up, inverse_up, normed_up = normalize(up_activation[0], upward_gain[0])
    hidden = normed_up.astype(jnp.bfloat16)
    key_value = lax.all_gather(saved[:, width:], "seq", axis=0, tiled=True)
    keys = key_value[:, :HEAD]
    values = key_value[:, HEAD:]
    query = saved[:, :width].reshape(count, GROUP, HEAD)
    hidden_cols = lax.all_to_all(hidden, "seq", split_axis=1, concat_axis=0, tiled=True)
    block = cotangent
    attn_grad = contract_last(
        block, lax.all_gather(up_output_weight[0], "seq", axis=1, tiled=True)
    ).astype(jnp.bfloat16)
    positions = first + jnp.arange(count, dtype=jnp.int32)
    key_positions = jnp.arange(keys.shape[0], dtype=jnp.int32)
    starts = doc_starts[0]
    visible = (key_positions[None, :] <= positions[:, None]) & (
        key_positions[None, :] >= starts[:, None]
    )
    scores = jnp.einsum("tgh,jh->tgj", query, keys, preferred_element_type=jnp.float32) * factor
    scores = jnp.where(visible[:, None, :], scores, -1e30)
    top = jnp.max(scores, axis=-1, keepdims=True)
    exps = jnp.where(visible[:, None, :], jnp.exp(scores - top), 0.0)
    probs = exps / jnp.sum(exps, axis=-1, keepdims=True)
    weights = probs.astype(jnp.bfloat16)
    grad_heads = attn_grad.reshape(count, GROUP, HEAD)
    prob_grad = jnp.einsum("tgh,jh->tgj", grad_heads, values, preferred_element_type=jnp.float32)
    inner = jnp.sum(probs * prob_grad, axis=-1, keepdims=True)
    score_grad = (probs * (prob_grad - inner) * factor).astype(jnp.bfloat16)
    query_grad = (
        jnp.einsum("tgj,jh->tgh", score_grad, keys, preferred_element_type=jnp.float32)
        .astype(jnp.bfloat16)
        .reshape(count, width)
    )
    key_part = jnp.einsum("tgj,tgh->jh", score_grad, query, preferred_element_type=jnp.float32)
    value_part = jnp.einsum("tgj,tgh->jh", weights, grad_heads, preferred_element_type=jnp.float32)
    key_total, value_total = (
        lax.psum(key_part.astype(jnp.bfloat16), "seq").astype(jnp.float32),
        lax.psum(value_part.astype(jnp.bfloat16), "seq").astype(jnp.float32),
    )
    kv_grad = jnp.concatenate(
        [key_total.astype(jnp.bfloat16), value_total.astype(jnp.bfloat16)], axis=1
    )
    query_all = lax.all_gather(query_grad, "seq", axis=0, tiled=True)
    grad_all = jnp.concatenate([query_all, kv_grad], axis=1)
    input_term = contract_first(hidden_cols, grad_all).astype(jnp.bfloat16)
    block = contract_last(grad_all, up_input_weight[0])
    hidden_grad = lax.all_to_all(block, "seq", split_axis=0, concat_axis=1, tiled=True)
    scaled = hidden_grad * upward_gain[0]
    input_grad = cotangent.astype(jnp.float32) + inverse_up * (
        scaled - unit_up * jnp.mean(scaled * unit_up, axis=-1, keepdims=True)
    )
    moved_grad = shifted(input_grad.astype(jnp.bfloat16), "section", 1)
    sections = lax.axis_size("section")
    mirror_input = input_term
    for bit in range(sections.bit_length() - 1):
        mirror_input = from_partner(mirror_input, "section", bit)
    project_grads = (accum_input[0].astype(jnp.float32) + mirror_input.astype(jnp.float32)).astype(
        jnp.bfloat16
    )
    return (moved_grad[None], project_grads[None])


def solution(mesh):
    return jax.shard_map(
        per_device,
        mesh=mesh,
        in_specs=(
            P("section", "seq", None),
            P("section", "seq", None),
            P("section", "seq", None),
            P("section", "seq", None),
            P("section", None, "seq"),
            P("section", None),
            P("section", "seq", None),
            P("section", "seq"),
        ),
        out_specs=(P("section", "seq", None), P("section", "seq", None)),
        check_vma=False,
    )
```

profile of v0, /device:TPU:25, one launch (start us, length us, event | category | flops | bytes accessed | tf_op | source)
XLA Modules:
  0.0 827.4 jit_solution(4818707884297721254)
XLA Ops:
  7.2 1.5 slice.17
  8.8 0.7 all-gather.9.cloned.1.call-update
  9.6 1.1 fusion.37
  10.7 82.6 %all-gather.5.cloned.1.call-done = bf16[2048,256]{1,0:T(8,128)(2,1)} async-done(((bf16[128,256]{1,0:T(8,128)(2,1)}), bf16[2048,256]{1,0:T(8,128)(2,1)}) %all-gather.5.cloned.1.call-update) | async-done | bytes 1048592 | tf_op jit(solution)/shard_map/all_gather | solution.py:57
  93.3 5.0 fusion.64
  98.4 136.5 %all-gather.9.cloned.1.call-done = bf16[1,512,4096]{2,1,0:T(8,128)(2,1)} async-done(((bf16[1,512,256]{2,1,0:T(8,128)(2,1)}), bf16[1,512,4096]{2,1,0:T(8,128)(2,1)}) %all-gather.9.cloned.1.call-update) | async-done | bytes 4194320 | tf_op jit(solution)/shard_map/all_gather | solution.py:64
  234.9 3.9 fusion.33
  238.8 1.8 fusion.9
  240.5 2.7 fusion.41
  243.2 8.2 fusion.8
  251.4 0.0 all-gather.7.cloned.1.call-start
  251.5 9.2 %fusion.27 = bf16[128,4,128]{0,2,1:T(8,128)(2,1)} fusion(f32[128,4,2048]{2,0,1:T(8,128)} %fusion.41, bf16[2048,256]{1,0:T(8,128)(2,1)S(1)} %copy-done.6, f32[128,4,2048]{2,0,1:T(8,128)} %get-tuple-element.9, f32[128,4]{0,1:T(4,128)S(1)} %get-tuple-element.8), kind=kOutput, calls=%fused_computation.35 | convolution fusion | flops 275843584 | bytes 17436672 | tf_op jit(solution)/shard_map/tgj,jh->tgh/dot_general | solution.py:83
  260.7 195.4 %all-reduce.3.cloned.1.call-done = (bf16[2048,128]{1,0:T(8,128)(2,1)}, bf16[2048,128]{1,0:T(8,128)(2,1)}) async-done(((bf16[2048,128]{1,0:T(8,128)(2,1)}, bf16[2048,128]{1,0:T(8,128)(2,1)}), (bf16[2048,128]{1,0:T(8,128)(2,1)}, bf16[2048,128]{1,0:T(8,128)(2,1)})) %all-reduce.3.cloned.1.call-update) | async-done | bytes 1048592 | tf_op jit(solution)/shard_map/psum | solution.py:91
  456.1 2.0 copy.29
  458.2 2.0 copy.30
  460.2 102.7 %all-gather.7.cloned.1.call-done = bf16[2048,512]{0,1:T(8,128)(2,1)} async-done(((bf16[128,512]{0,1:T(8,128)(2,1)}), bf16[2048,512]{0,1:T(8,128)(2,1)}) %all-gather.7.cloned.1.call-update) | async-done | bytes 2097168 | tf_op jit(solution)/shard_map/all_gather | solution.py:96
  562.9 2.0 pad_maximum_fusion
  565.0 2.8 copy.31
  567.8 4.2 fusion.43
  572.1 10.1 %all-to-all-start = ((f32[16,128,256]{2,1,0:T(8,128)}), f32[16,128,256]{2,1,0:T(8,128)S(1)}, u32[]{:S(2)}, u32[]{:S(2)}) async-start(f32[16,128,256]{2,1,0:T(8,128)} %fusion.43), calls=%async_computation | async-start | bytes 4194304 | tf_op jit(solution)/shard_map/all_to_all | solution.py:100
  582.2 1.6 copy.21
  583.8 1.6 copy.33
  585.5 0.6 broadcast.82
  586.0 1.3 reduce.4
  587.4 1.3 mul.85
  588.7 0.6 fusion.19
  589.2 0.5 add_rsqrt_fusion
  589.8 73.2 %all-to-all-done = f32[16,128,256]{2,1,0:T(8,128)S(1)} async-done(((f32[16,128,256]{2,1,0:T(8,128)}), f32[16,128,256]{2,1,0:T(8,128)S(1)}, u32[]{:S(2)}, u32[]{:S(2)}) %all-to-all-start) | async-done | bytes 2097184 | tf_op jit(solution)/shard_map/all_to_all | solution.py:100
  662.9 3.1 multiply_convert_fusion.1
  666.0 76.9 %all_to_all.32 = bf16[128,16,256]{2,0,1:T(8,128)(2,1)S(1)} all-to-all(bf16[128,16,256]{2,0,1:T(8,128)(2,1)S(1)} %get-tuple-element.6), channel_id=1, replica_groups=mesh['section'=32,'seq'=16] {'seq'}, dimensions={1} | all-to-all | bytes 2097152 | tf_op jit(solution)/shard_map/all_to_all | solution.py:61
  742.9 1.0 convolution_convert_fusion
  743.9 5.6 collective-permute-start.1
  749.5 1.5 collective-permute-done.1
  751.0 1.9 collective-permute-start.2
  752.9 2.3 copy.20
  755.2 1.8 copy.32
  757.0 0.7 broadcast_multiply_fusion
  757.8 5.8 collective-permute-done.2
  763.5 1.9 collective-permute-start.3
  765.4 2.3 fusion.18
  767.7 1.9 collective-permute-start
  769.7 6.8 collective-permute-done.3
  776.5 8.9 %collective-permute-start.4 = (bf16[256,768]{1,0:T(8,128)(2,1)S(1)}, bf16[256,768]{1,0:T(8,128)(2,1)S(1)}, u32[]{:S(2)}, u32[]{:S(2)}) collective-permute-start(bf16[256,768]{1,0:T(8,128)(2,1)S(1)} %collective-permute-done.3), channel_id=1, source_target_pairs={{0,128},{16,144},{32,160},{48,176},{64,192},{80,208},{96,224},{112... | collective-permute-start | bytes 1179656 | tf_op jit(solution)/shard_map/ppermute | solution.py:17
  785.4 6.4 collective-permute-done.4
  791.8 11.7 %collective-permute-start.5 = (bf16[256,768]{1,0:T(8,128)(2,1)S(1)}, bf16[256,768]{1,0:T(8,128)(2,1)S(1)}, u32[]{:S(2)}, u32[]{:S(2)}) collective-permute-start(bf16[256,768]{1,0:T(8,128)(2,1)S(1)} %collective-permute-done.4), channel_id=1, source_target_pairs={{0,256},{16,272},{32,288},{48,304},{64,320},{80,336},{96,352},{112... | collective-permute-start | bytes 1179656 | tf_op jit(solution)/shard_map/ppermute | solution.py:17
  803.5 1.3 copy.34
  804.8 15.2 %collective-permute-done.5 = bf16[256,768]{1,0:T(8,128)(2,1)S(1)} collective-permute-done((bf16[256,768]{1,0:T(8,128)(2,1)S(1)}, bf16[256,768]{1,0:T(8,128)(2,1)S(1)}, u32[]{:S(2)}, u32[]{:S(2)}) %collective-permute-start.5) | collective-permute-done | bytes 393248 | tf_op jit(solution)/shard_map/ppermute | solution.py:17
  820.1 0.8 fusion.42
  (28 shorter events, 0.2 us)
Async XLA Ops:
  7.2 560.7 %copy-start = (bf16[1,256,768]{2,1,0:T(8,128)(2,1)S(1)}, bf16[1,256,768]{2,1,0:T(8,128)(2,1)}, u32[]{:S(2)}) copy-start(bf16[1,256,768]{2,1,0:T(8,128)(2,1)} %param.11) | copy-start | bytes 1179652
  7.2 86.2 %all-gather.5.cloned.1.call-start = ((), (), s32[]{:S(2)}) async-start(), calls=%async_computation.2 | async-start | bytes 1114112 | tf_op jit(solution)/shard_map/all_gather | solution.py:57
  8.8 226.1 %all-gather.9.cloned.1.call-start = ((), (), s32[]{:S(2)}) async-start(), calls=%async_computation.4 | async-start | bytes 4456448 | tf_op jit(solution)/shard_map/all_gather | solution.py:64
  9.5 446.6 %all-reduce.3.cloned.1.call-start = ((), (), s32[]{:S(2)}) async-start(), calls=%async_computation.5 | async-start | bytes 2097152 | tf_op jit(solution)/shard_map/psum | solution.py:91
  10.7 224.2 %copy-start.1 = (bf16[1,128,4096]{2,1,0:T(8,128)(2,1)S(1)}, bf16[1,128,4096]{2,1,0:T(8,128)(2,1)}, u32[]{:S(2)}) copy-start(bf16[1,128,4096]{2,1,0:T(8,128)(2,1)} %param.10) | copy-start | bytes 3145732
  234.9 3.9 copy-start.9
  238.8 1.8 copy-start.6
  240.5 2.7 copy-start.8
  251.4 311.5 %all-gather.7.cloned.1.call-start = ((), (), s32[]{:S(2)}) async-start(), calls=%async_computation.3 | async-start | bytes 2228224 | tf_op jit(solution)/shard_map/all_gather | solution.py:96
  572.1 14.0 %copy-start.7 = (f32[1,4096]{1,0:T(1,128)S(1)}, f32[1,4096]{1,0:T(1,128)}, u32[]{:S(2)}) copy-start(f32[1,4096]{1,0:T(1,128)} %param.13) | copy-start | bytes 49156
  572.1 90.9 %all-to-all-start = ((f32[16,128,256]{2,1,0:T(8,128)}), f32[16,128,256]{2,1,0:T(8,128)S(1)}, u32[]{:S(2)}, u32[]{:S(2)}) async-start(f32[16,128,256]{2,1,0:T(8,128)} %fusion.43), calls=%async_computation | async-start | bytes 4194304 | tf_op jit(solution)/shard_map/all_to_all | solution.py:100
  662.9 80.0 %copy-start.2 = (bf16[2048,512]{0,1:T(8,128)(2,1)S(1)}, bf16[2048,512]{0,1:T(8,128)(2,1)}, u32[]{:S(2)}) copy-start(bf16[2048,512]{0,1:T(8,128)(2,1)} %all-gather.7.cloned.1.call-done) | copy-start | bytes 6291460
  662.9 80.0 %copy-start.3 = (bf16[2048,128]{0,1:T(8,128)(2,1)S(1)}, bf16[2048,128]{0,1:T(8,128)(2,1)}, u32[]{:S(2)}) copy-start(bf16[2048,128]{0,1:T(8,128)(2,1)} %copy.29) | copy-start | bytes 1572868
  662.9 80.0 %copy-start.4 = (bf16[2048,128]{0,1:T(8,128)(2,1)S(1)}, bf16[2048,128]{0,1:T(8,128)(2,1)}, u32[]{:S(2)}) copy-start(bf16[2048,128]{0,1:T(8,128)(2,1)} %copy.30) | copy-start | bytes 1572868
  743.9 7.1 collective-permute-start.1
  751.0 12.5 %collective-permute-start.2 = (bf16[256,768]{1,0:T(8,128)(2,1)}, bf16[256,768]{1,0:T(8,128)(2,1)}, u32[]{:S(2)}, u32[]{:S(2)}) collective-permute-start(bf16[256,768]{1,0:T(8,128)(2,1)} %collective-permute-done.1), channel_id=1, source_target_pairs={{0,32},{16,48},{32,0},{48,16},{64,96},{80,112},{96,64},{112,80},{1... | collective-permute-start | bytes 1179656 | tf_op jit(solution)/shard_map/ppermute | solution.py:17
  757.0 63.1 %copy-start.5 = (bf16[1,256,768]{2,1,0:T(8,128)(2,1)S(1)}, bf16[1,256,768]{2,1,0:T(8,128)(2,1)}, u32[]{:S(2)}) copy-start(bf16[1,256,768]{2,1,0:T(8,128)(2,1)} %param.14) | copy-start | bytes 1179652
  763.5 13.0 %collective-permute-start.3 = (bf16[256,768]{1,0:T(8,128)(2,1)}, bf16[256,768]{1,0:T(8,128)(2,1)S(1)}, u32[]{:S(2)}, u32[]{:S(2)}) collective-permute-start(bf16[256,768]{1,0:T(8,128)(2,1)} %collective-permute-done.2), channel_id=1, source_target_pairs={{0,64},{16,80},{32,96},{48,112},{64,0},{80,16},{96,32},{112,48},{1... | collective-permute-start | bytes 1179656 | tf_op jit(solution)/shard_map/ppermute | solution.py:17
  767.7 35.8 %collective-permute-start = (bf16[128,4096]{0,1:T(8,128)(2,1)S(1)}, bf16[128,4096]{0,1:T(8,128)(2,1)S(1)}, u32[]{:S(2)}, u32[]{:S(2)}) collective-permute-start(bf16[128,4096]{0,1:T(8,128)(2,1)S(1)} %fusion.18), channel_id=1, source_target_pairs={{0,16},{16,32},{32,48},{48,64},{64,80},{80,96},{96,112},{112,128},... | collective-permute-start | bytes 3145736 | tf_op jit(solution)/shard_map/ppermute | solution.py:13
  776.5 15.3 %collective-permute-start.4 = (bf16[256,768]{1,0:T(8,128)(2,1)S(1)}, bf16[256,768]{1,0:T(8,128)(2,1)S(1)}, u32[]{:S(2)}, u32[]{:S(2)}) collective-permute-start(bf16[256,768]{1,0:T(8,128)(2,1)S(1)} %collective-permute-done.3), channel_id=1, source_target_pairs={{0,128},{16,144},{32,160},{48,176},{64,192},{80,208},{96,224},{112... | collective-permute-start | bytes 1179656 | tf_op jit(solution)/shard_map/ppermute | solution.py:17
  791.8 28.2 %collective-permute-start.5 = (bf16[256,768]{1,0:T(8,128)(2,1)S(1)}, bf16[256,768]{1,0:T(8,128)(2,1)S(1)}, u32[]{:S(2)}, u32[]{:S(2)}) collective-permute-start(bf16[256,768]{1,0:T(8,128)(2,1)S(1)} %collective-permute-done.4), channel_id=1, source_target_pairs={{0,256},{16,272},{32,288},{48,304},{64,320},{80,336},{96,352},{112... | collective-permute-start | bytes 1179656 | tf_op jit(solution)/shard_map/ppermute | solution.py:17
Sparse Core Ops, SparseCore 0:
  11.6 81.7 all-gather.4
  96.3 138.4 all-gather.8
  251.5 204.5 all-reduce.2
  460.0 102.9 all-gather.6
where the time goes:
time: 828 us; the launch traced here: 827 us
  waiting for transfers between devices  627 us (76%)
  blocking collectives  76.9 us (9%)
  starting transfers between devices  42.2 us (5%)
  matrix products  36 us (4%)
  local copies, waits for them, and re-layouts  19.1 us (2%)
  between operations  13.9 us (2%)
  other arithmetic  12.5 us (2%)
    psum x1, waiting for transfers between devices, per_device(): lax.psum(value_part.astype(jnp.bfloat16), 'seq').astype(jnp.float32)  195 us
    all_gather x1, waiting for transfers between devices, per_device(): lax.all_gather(up_output_weight[0], 'seq', axis=1, tiled=True)  137 us
    all_gather x1, waiting for transfers between devices, per_device(): query_all = lax.all_gather(query_grad, 'seq', axis=0, tiled=True)  103 us
    all_gather x1, waiting for transfers between devices, per_device(): key_value = lax.all_gather(saved[:, width:], 'seq', axis=0, tiled=True)  82.6 us
    all_to_all x1, blocking collectives, per_device(): lax.all_to_all(hidden, 'seq', split_axis=1, concat_axis=0, tiled=True)  76.9 us
    all_to_all x1, waiting for transfers between devices, per_device(): lax.all_to_all(block, 'seq', split_axis=0, concat_axis=1, tiled=True)  73.2 us
    ppermute x5, waiting for transfers between devices, from_partner(): lax.ppermute(x, axis, [(i, i ^ 1 << stride) for i in range(lax.axis_size(...  35.7 us
    ppermute x5, starting transfers between devices, from_partner(): lax.ppermute(x, axis, [(i, i ^ 1 << stride) for i in range(lax.axis_size(...  30 us
  transfers between devices with their start and end apart: 11, of which 10 were waited for; matrix products, arithmetic and copies ran while one was open for 4% of the time, Pallas kernels for 0%

commit v1 on v0

--- a/solution.py
+++ b/solution.py
@@ -97,7 +97,10 @@
     grad_all = jnp.concatenate([query_all, kv_grad], axis=1)
     input_term = contract_first(hidden_cols, grad_all).astype(jnp.bfloat16)
     block = contract_last(grad_all, up_input_weight[0])
-    hidden_grad = lax.all_to_all(block, "seq", split_axis=0, concat_axis=1, tiled=True)
+    hidden_grad = jnp.concatenate(
+        lax.all_to_all(jnp.stack(jnp.split(block, lax.axis_size("seq"), axis=0)), "seq", 0, 0),
+        axis=1,
+    )
     scaled = hidden_grad * upward_gain[0]
     input_grad = cotangent.astype(jnp.float32) + inverse_up * (
         scaled - unit_up * jnp.mean(scaled * unit_up, axis=-1, keepdims=True)

time: 828 us -> 833 us (level)
    unnamed x24 -> x43, local copies, waits for them, and re-layouts: 5.81 us -> 15.8 us
where the time goes in v1:
time: 833 us; the launch traced here: 832 us
  waiting for transfers between devices  634 us (76%)
  blocking collectives  72 us (9%)
  starting transfers between devices  42.4 us (5%)
  matrix products  34.4 us (4%)
  local copies, waits for them, and re-layouts  25.4 us (3%)
  between operations  14 us (2%)
  other arithmetic  10.4 us (1%)
    psum x1, waiting for transfers between devices, per_device(): lax.psum(value_part.astype(jnp.bfloat16), 'seq').astype(jnp.float32)  196 us
    all_gather x1, waiting for transfers between devices, per_device(): lax.all_gather(up_output_weight[0], 'seq', axis=1, tiled=True)  137 us
    all_gather x1, waiting for transfers between devices, per_device(): query_all = lax.all_gather(query_grad, 'seq', axis=0, tiled=True)  104 us
    all_gather x1, waiting for transfers between devices, per_device(): key_value = lax.all_gather(saved[:, width:], 'seq', axis=0, tiled=True)  82.6 us
    all_to_all x1, waiting for transfers between devices, per_device(): lax.all_to_all(jnp.stack(jnp.split(block, lax.axis_size('seq'), axis=0)),...  73 us
    all_to_all x1, blocking collectives, per_device(): lax.all_to_all(hidden, 'seq', split_axis=1, concat_axis=0, tiled=True)  72 us
    ppermute x5, waiting for transfers between devices, from_partner(): lax.ppermute(x, axis, [(i, i ^ 1 << stride) for i in range(lax.axis_size(...  40.8 us
    ppermute x5, starting transfers between devices, from_partner(): lax.ppermute(x, axis, [(i, i ^ 1 << stride) for i in range(lax.axis_size(...  30.2 us
  transfers between devices with their start and end apart: 11, of which 10 were waited for; matrix products, arithmetic and copies ran while one was open for 4% of the time, Pallas kernels for 0%

profile of v1, /device:TPU:25, one launch (start us, length us, event | category | flops | bytes accessed | tf_op | source)
XLA Modules:
  0.0 832.2 jit_solution(3859883911633951764)
XLA Ops:
  7.2 1.5 slice.17
  8.8 0.7 all-gather.9.cloned.1.call-update
  9.6 1.1 fusion.40
  10.7 82.6 %all-gather.5.cloned.1.call-done = bf16[2048,256]{1,0:T(8,128)(2,1)} async-done(((bf16[128,256]{1,0:T(8,128)(2,1)}), bf16[2048,256]{1,0:T(8,128)(2,1)}) %all-gather.5.cloned.1.call-update) | async-done | bytes 1048592 | tf_op jit(solution)/shard_map/all_gather | solution.py:57
  93.3 5.0 fusion.84
  98.4 136.5 %all-gather.9.cloned.1.call-done = bf16[1,512,4096]{2,1,0:T(8,128)(2,1)} async-done(((bf16[1,512,256]{2,1,0:T(8,128)(2,1)}), bf16[1,512,4096]{2,1,0:T(8,128)(2,1)}) %all-gather.9.cloned.1.call-update) | async-done | bytes 4194320 | tf_op jit(solution)/shard_map/all_gather | solution.py:64
  234.9 3.9 fusion.36
  238.8 1.8 fusion.9
  240.5 2.7 fusion.44
  243.2 8.2 fusion.8
  251.5 9.2 %fusion.30 = bf16[128,4,128]{0,2,1:T(8,128)(2,1)} fusion(f32[128,4,2048]{2,0,1:T(8,128)} %fusion.44, bf16[2048,256]{1,0:T(8,128)(2,1)S(1)} %copy-done.7, f32[128,4,2048]{2,0,1:T(8,128)} %get-tuple-element.9, f32[128,4]{0,1:T(4,128)S(1)} %get-tuple-element.8), kind=kOutput, calls=%fused_computation.37 | convolution fusion | flops 275843584 | bytes 17436672 | tf_op jit(solution)/shard_map/tgj,jh->tgh/dot_general | solution.py:83
  260.7 195.8 %all-reduce.3.cloned.1.call-done = (bf16[2048,128]{1,0:T(8,128)(2,1)}, bf16[2048,128]{1,0:T(8,128)(2,1)}) async-done(((bf16[2048,128]{1,0:T(8,128)(2,1)}, bf16[2048,128]{1,0:T(8,128)(2,1)}), (bf16[2048,128]{1,0:T(8,128)(2,1)}, bf16[2048,128]{1,0:T(8,128)(2,1)})) %all-reduce.3.cloned.1.call-update) | async-done | bytes 1048592 | tf_op jit(solution)/shard_map/psum | solution.py:91
  456.6 1.2 copy.28
  457.8 1.4 copy.29
  459.3 104.1 %all-gather.7.cloned.1.call-done = bf16[2048,512]{0,1:T(8,128)(2,1)} async-done(((bf16[128,512]{0,1:T(8,128)(2,1)}), bf16[2048,512]{0,1:T(8,128)(2,1)}) %all-gather.7.cloned.1.call-update) | async-done | bytes 2097168 | tf_op jit(solution)/shard_map/all_gather | solution.py:96
  563.4 2.7 fusion.28
  568.7 0.7 fusion.65
  569.4 0.7 fusion.64
  570.0 0.7 fusion.63
  573.4 0.7 fusion.58
  574.7 0.7 fusion.56
  575.4 0.7 fusion.55
  576.7 10.0 %all-to-all-start = ((f32[16,128,256]{2,1,0:T(8,128)}), f32[16,128,256]{2,1,0:T(8,128)S(1)}, u32[]{:S(2)}, u32[]{:S(2)}) async-start(f32[16,128,256]{2,1,0:T(8,128)} %fusion.54), calls=%async_computation | async-start | bytes 4194304 | tf_op jit(solution)/shard_map/all_to_all | solution.py:101
  586.7 1.6 copy.20
  588.4 1.6 copy.31
  590.5 1.3 reduce.4
  591.8 1.3 mul.85
  594.2 73.0 %all-to-all-done = f32[16,128,256]{2,1,0:T(8,128)S(1)} async-done(((f32[16,128,256]{2,1,0:T(8,128)}), f32[16,128,256]{2,1,0:T(8,128)S(1)}, u32[]{:S(2)}, u32[]{:S(2)}) %all-to-all-start) | async-done | bytes 2097184 | tf_op jit(solution)/shard_map/all_to_all | solution.py:101
  667.2 3.1 multiply_convert_fusion.1
  670.2 72.0 %all_to_all.21 = bf16[128,16,256]{2,0,1:T(8,128)(2,1)S(1)} all-to-all(bf16[128,16,256]{2,0,1:T(8,128)(2,1)S(1)} %get-tuple-element.6), channel_id=1, replica_groups=mesh['section'=32,'seq'=16] {'seq'}, dimensions={1} | all-to-all | bytes 2097152 | tf_op jit(solution)/shard_map/all_to_all | solution.py:61
  742.3 1.0 fusion.29
  743.3 4.8 collective-permute-start.1
  748.1 1.5 collective-permute-done.1
  749.5 4.2 collective-permute-start.2
  753.7 2.3 copy.19
  756.0 1.8 copy.30
  757.8 0.7 broadcast_multiply_fusion
  758.5 4.7 collective-permute-done.2
  763.2 16.3 %collective-permute-start.3 = (bf16[256,768]{1,0:T(8,128)(2,1)}, bf16[256,768]{1,0:T(8,128)(2,1)S(1)}, u32[]{:S(2)}, u32[]{:S(2)}) collective-permute-start(bf16[256,768]{1,0:T(8,128)(2,1)} %collective-permute-done.2), channel_id=1, source_target_pairs={{0,64},{16,80},{32,96},{48,112},{64,0},{80,16},{96,32},{112,48},{1... | collective-permute-start | bytes 1179656 | tf_op jit(solution)/shard_map/ppermute | solution.py:17
  779.5 2.3 fusion.18
  781.9 2.1 collective-permute-start
  783.9 4.1 collective-permute-done.3
  788.0 2.3 collective-permute-start.4
  790.3 13.8 %collective-permute-done.4 = bf16[256,768]{1,0:T(8,128)(2,1)S(1)} collective-permute-done((bf16[256,768]{1,0:T(8,128)(2,1)S(1)}, bf16[256,768]{1,0:T(8,128)(2,1)S(1)}, u32[]{:S(2)}, u32[]{:S(2)}) %collective-permute-start.4) | collective-permute-done | bytes 393248 | tf_op jit(solution)/shard_map/ppermute | solution.py:17
  804.1 2.6 collective-permute-start.5
  806.7 1.3 copy.32
  808.0 16.8 %collective-permute-done.5 = bf16[256,768]{1,0:T(8,128)(2,1)S(1)} collective-permute-done((bf16[256,768]{1,0:T(8,128)(2,1)S(1)}, bf16[256,768]{1,0:T(8,128)(2,1)S(1)}, u32[]{:S(2)}, u32[]{:S(2)}) %collective-permute-start.5) | collective-permute-done | bytes 393248 | tf_op jit(solution)/shard_map/ppermute | solution.py:17
  824.8 0.8 fusion.45
  (46 shorter events, 8.5 us)
Async XLA Ops:
  7.2 556.2 %copy-start = (bf16[1,256,768]{2,1,0:T(8,128)(2,1)S(1)}, bf16[1,256,768]{2,1,0:T(8,128)(2,1)}, u32[]{:S(2)}) copy-start(bf16[1,256,768]{2,1,0:T(8,128)(2,1)} %param.11) | copy-start | bytes 1179652
  7.2 86.2 %all-gather.5.cloned.1.call-start = ((), (), s32[]{:S(2)}) async-start(), calls=%async_computation.2 | async-start | bytes 1114112 | tf_op jit(solution)/shard_map/all_gather | solution.py:57
  8.8 226.1 %all-gather.9.cloned.1.call-start = ((), (), s32[]{:S(2)}) async-start(), calls=%async_computation.4 | async-start | bytes 4456448 | tf_op jit(solution)/shard_map/all_gather | solution.py:64
  9.5 447.0 %all-reduce.3.cloned.1.call-start = ((), (), s32[]{:S(2)}) async-start(), calls=%async_computation.5 | async-start | bytes 2097152 | tf_op jit(solution)/shard_map/psum | solution.py:91
  10.7 224.2 %copy-start.1 = (bf16[1,128,4096]{2,1,0:T(8,128)(2,1)S(1)}, bf16[1,128,4096]{2,1,0:T(8,128)(2,1)}, u32[]{:S(2)}) copy-start(bf16[1,128,4096]{2,1,0:T(8,128)(2,1)} %param.10) | copy-start | bytes 3145732
  234.9 3.9 copy-start.11
  238.8 1.8 copy-start.7
  240.5 2.7 copy-start.9
  251.4 312.0 %all-gather.7.cloned.1.call-start = ((), (), s32[]{:S(2)}) async-start(), calls=%async_computation.3 | async-start | bytes 2228224 | tf_op jit(solution)/shard_map/all_gather | solution.py:96
  457.8 108.2 %copy-start.2 = (bf16[2048,128]{0,1:T(8,128)(2,1)}, bf16[2048,128]{0,1:T(8,128)(2,1)S(1)}, u32[]{:S(2)}) copy-start(bf16[2048,128]{0,1:T(8,128)(2,1)S(1)} %copy.28) | copy-start | bytes 1572868
  459.3 106.8 %copy-start.4 = (bf16[2048,128]{0,1:T(8,128)(2,1)}, bf16[2048,128]{0,1:T(8,128)(2,1)S(1)}, u32[]{:S(2)}) copy-start(bf16[2048,128]{0,1:T(8,128)(2,1)S(1)} %copy.29) | copy-start | bytes 1572868
  576.7 90.4 %all-to-all-start = ((f32[16,128,256]{2,1,0:T(8,128)}), f32[16,128,256]{2,1,0:T(8,128)S(1)}, u32[]{:S(2)}, u32[]{:S(2)}) async-start(f32[16,128,256]{2,1,0:T(8,128)} %fusion.54), calls=%async_computation | async-start | bytes 4194304 | tf_op jit(solution)/shard_map/all_to_all | solution.py:101
  588.4 2.2 copy-start.8
  667.2 75.1 %copy-start.10 = (bf16[2048,512]{0,1:T(8,128)(2,1)S(1)}, bf16[2048,512]{0,1:T(8,128)(2,1)}, u32[]{:S(2)}) copy-start(bf16[2048,512]{0,1:T(8,128)(2,1)} %all-gather.7.cloned.1.call-done) | copy-start | bytes 6291460
  670.2 72.0 %copy-start.3 = (bf16[2048,128]{0,1:T(8,128)(2,1)S(1)}, bf16[2048,128]{0,1:T(8,128)(2,1)}, u32[]{:S(2)}) copy-start(bf16[2048,128]{0,1:T(8,128)(2,1)} %copy-done.2) | copy-start | bytes 1572868
  670.2 72.0 %copy-start.5 = (bf16[2048,128]{0,1:T(8,128)(2,1)S(1)}, bf16[2048,128]{0,1:T(8,128)(2,1)}, u32[]{:S(2)}) copy-start(bf16[2048,128]{0,1:T(8,128)(2,1)} %copy-done.4) | copy-start | bytes 1572868
  743.3 6.2 collective-permute-start.1
  749.5 13.6 %collective-permute-start.2 = (bf16[256,768]{1,0:T(8,128)(2,1)}, bf16[256,768]{1,0:T(8,128)(2,1)}, u32[]{:S(2)}, u32[]{:S(2)}) collective-permute-start(bf16[256,768]{1,0:T(8,128)(2,1)} %collective-permute-done.1), channel_id=1, source_target_pairs={{0,32},{16,48},{32,0},{48,16},{64,96},{80,112},{96,64},{112,80},{1... | collective-permute-start | bytes 1179656 | tf_op jit(solution)/shard_map/ppermute | solution.py:17
  763.2 24.8 %collective-permute-start.3 = (bf16[256,768]{1,0:T(8,128)(2,1)}, bf16[256,768]{1,0:T(8,128)(2,1)S(1)}, u32[]{:S(2)}, u32[]{:S(2)}) collective-permute-start(bf16[256,768]{1,0:T(8,128)(2,1)} %collective-permute-done.2), channel_id=1, source_target_pairs={{0,64},{16,80},{32,96},{48,112},{64,0},{80,16},{96,32},{112,48},{1... | collective-permute-start | bytes 1179656 | tf_op jit(solution)/shard_map/ppermute | solution.py:17
  781.8 43.0 %copy-start.6 = (bf16[1,256,768]{2,1,0:T(8,128)(2,1)S(1)}, bf16[1,256,768]{2,1,0:T(8,128)(2,1)}, u32[]{:S(2)}) copy-start(bf16[1,256,768]{2,1,0:T(8,128)(2,1)} %param.14) | copy-start | bytes 1179652
  781.9 24.8 %collective-permute-start = (bf16[128,4096]{0,1:T(8,128)(2,1)S(1)}, bf16[128,4096]{0,1:T(8,128)(2,1)S(1)}, u32[]{:S(2)}, u32[]{:S(2)}) collective-permute-start(bf16[128,4096]{0,1:T(8,128)(2,1)S(1)} %fusion.18), channel_id=1, source_target_pairs={{0,16},{16,32},{32,48},{48,64},{64,80},{80,96},{96,112},{112,128},... | collective-permute-start | bytes 3145736 | tf_op jit(solution)/shard_map/ppermute | solution.py:13
  788.0 16.1 %collective-permute-start.4 = (bf16[256,768]{1,0:T(8,128)(2,1)S(1)}, bf16[256,768]{1,0:T(8,128)(2,1)S(1)}, u32[]{:S(2)}, u32[]{:S(2)}) collective-permute-start(bf16[256,768]{1,0:T(8,128)(2,1)S(1)} %collective-permute-done.3), channel_id=1, source_target_pairs={{0,128},{16,144},{32,160},{48,176},{64,192},{80,208},{96,224},{112... | collective-permute-start | bytes 1179656 | tf_op jit(solution)/shard_map/ppermute | solution.py:17
  804.1 20.7 %collective-permute-start.5 = (bf16[256,768]{1,0:T(8,128)(2,1)S(1)}, bf16[256,768]{1,0:T(8,128)(2,1)S(1)}, u32[]{:S(2)}, u32[]{:S(2)}) collective-permute-start(bf16[256,768]{1,0:T(8,128)(2,1)S(1)} %collective-permute-done.4), channel_id=1, source_target_pairs={{0,256},{16,272},{32,288},{48,304},{64,320},{80,336},{96,352},{112... | collective-permute-start | bytes 1179656 | tf_op jit(solution)/shard_map/ppermute | solution.py:17
Sparse Core Ops, SparseCore 0:
  11.6 81.7 all-gather.4
  96.3 138.4 all-gather.8
  251.5 204.9 all-reduce.2
  460.4 102.9 all-gather.6
